TPU v7x, 512 devices: a whole 4x8x8 slice. The times are simulated.
512 devices in a mesh: tm: 16 (over y, core), pre: 32 (over z, x).
Axes of the slice: x: 4, y: 8, z: 8, core: 2. Of those that a mesh axis runs over, the one named last changes fastest.
Arguments:
- spikes: int32 [3072, 16384], P('tm', 'pre'), may hold values from 0 to 1
- trace_decay: float32 [16384], P('pre'), may hold values from 0.96 to 1
- pseudo_deriv: bfloat16 [3072, 16384], P('pre', 'tm'), may hold values from 0 to 0.29882812
- readout_weight: bfloat16 [16384, 512], P('pre'), may hold values from -2 to 2
- feedback_weight: bfloat16 [16384, 512], P('tm'), may hold values from -6 to 6
- targets: int32 [3072], P('tm'), may hold values from 0 to 511
Outputs:
- gradient: float32 [16384, 16384], P('pre', 'tm')
All inputs are finite; a program needn't handle non-finite values.
Results may differ from a plain program's by a relative error of at most 0.0022.
Values may be sent and summed in bfloat16 or wider, within the bound.
No kernel may reach another device: no remote copies, remote signals or barrier semaphores. Data moves between devices by JAX's collectives and lax.ppermute only.
A program may use at most 64 MiB of HBM per device.

v0:
```python
import jax
import jax.numpy as jnp
from jax import lax
from jax.sharding import PartitionSpec as P


def prefix(value, axis, combine, identity):
    count, index = (lax.axis_size(axis), lax.axis_index(axis))
    everything = jax.tree.map(lambda part: lax.all_gather(part, axis), value)
    start = jax.tree.map(
        lambda part, zero: jnp.broadcast_to(jnp.asarray(zero, part.dtype), part.shape),
        value,
        identity,
    )

    def step(k, before):
        reached = k < index
        new = combine(before, jax.tree.map(lambda part: part[k], everything))
        return jax.tree.map(lambda a, b: jnp.where(reached, a, b), new, before)

    return lax.fori_loop(0, count, step, start)


def combine_pairs(earlier, later):
    return (earlier[0] * later[0], later[1] + later[0] * earlier[1])


def local_traces(spikes, decays):
    factor = jnp.broadcast_to(decays[None, :], spikes.shape)
    source = (1.0 - decays)[None, :] * spikes.astype(jnp.float32)
    return lax.associative_scan(combine_pairs, (factor, source), axis=0)


def error_rows(spikes, readout_weight, targets):
    partial_logits = jnp.dot(
        spikes.astype(jnp.bfloat16), readout_weight, preferred_element_type=jnp.float32
    )
    logits = lax.psum(partial_logits, "pre")
    class_prob = jax.nn.softmax(logits, axis=-1)
    classes = lax.broadcasted_iota(jnp.int32, logits.shape, 1)
    onehot = (targets[:, None] == classes).astype(jnp.float32)
    return (class_prob - onehot).astype(jnp.bfloat16)


def make_signal(errors_all, feedback_weight, derivs, offset):
    err_rows = lax.dynamic_slice_in_dim(errors_all, offset, derivs.shape[0], 0)
    signal = lax.dot_general(
        err_rows, feedback_weight, (((1,), (1,)), ((), ())), preferred_element_type=jnp.float32
    )
    return (signal * derivs.astype(jnp.float32)).astype(jnp.bfloat16)


def outer_sum(left_rows, right_rows):
    return lax.dot_general(
        left_rows, right_rows, (((0,), (0,)), ((), ())), preferred_element_type=jnp.float32
    )


def shards(spikes, trace_decay, pseudo_deriv, readout_weight, feedback_weight, targets):
    errors = error_rows(spikes, readout_weight, targets)
    errors_all = lax.all_gather(errors, "tm", axis=0, tiled=True)
    powers, states = local_traces(spikes, trace_decay)
    carried = prefix(
        (powers[-1], states[-1]),
        "tm",
        combine_pairs,
        (jnp.ones_like(trace_decay), jnp.zeros_like(trace_decay)),
    )
    incoming = carried[1]
    traces = (states + powers * incoming[None, :]).astype(jnp.bfloat16)
    offset = lax.axis_index("pre") * pseudo_deriv.shape[0]
    sources = make_signal(errors_all, feedback_weight, pseudo_deriv, offset)
    signal_all = lax.all_gather(sources, "pre", axis=0, tiled=True)
    return outer_sum(lax.all_gather(traces, "tm", axis=0, tiled=True), signal_all)


def solution(mesh):
    placed = (P("tm", "pre"), P("pre"), P("pre", "tm"), P("pre", None), P("tm", None), P("tm"))
    return jax.shard_map(
        shards, mesh=mesh, in_specs=placed, out_specs=P("pre", "tm"), check_vma=False
    )
```

profile of v0, /device:TPU:1, one launch (start us, length us, event | category | flops | bytes accessed | tf_op | source)
XLA Modules:
  0.0 374.8 jit_solution(8021454056844879361)
XLA Ops:
  6.5 2.3 fusion.3
  8.8 0.0 all-reduce.30.cloned.1.call-update
  8.8 0.0 all-gather.8.cloned.1.call-start
  8.9 0.7 broadcast_subtract_fusion
  9.6 1.0 convert_multiply_fusion
  10.6 0.1 slice.194
  10.8 0.1 slice.192
  10.9 0.2 slice.190
  12.8 0.1 fusion.2
  12.9 0.2 slice-done
  13.2 0.1 pad.98
  13.3 0.1 pad.99
  13.3 20.9 %all-gather = f32[16,1,512]{2,1,0:T(1,128)S(1)} all-gather(f32[1,1,512]{2,1,0:T(1,128)S(1)} %add_bitcast_fusion.1), channel_id=1, replica_groups=mesh['tm'=16,'pre'=32] {'tm'}, dimensions={0}, use_global_device_ids=true | all-gather | bytes 34816 | tf_op jit(solution)/shard_map/all_gather | solution.py:9
  34.3 0.1 pad.113
  34.4 0.1 pad.112
  34.4 134.3 %all-reduce.30.cloned.1.call-done = f32[192,512]{1,0:T(8,128)} async-done(((f32[192,512]{1,0:T(8,128)}), f32[192,512]{1,0:T(8,128)}) %all-reduce.30.cloned.1.call-update) | async-done | bytes 393232 | tf_op jit(solution)/shard_map/psum | solution.py:38
  168.8 1.1 reduce_max.9
  169.9 1.2 fusion.1
  171.1 1.9 subtract_convert_fusion
  173.0 0.0 all-gather.8.cloned.1.call-update
  173.0 0.0 all-gather.6.cloned.1.call-start
  173.0 22.0 %all-gather.1 = f32[16,1,512]{2,1,0:T(1,128)S(1)} all-gather(f32[1,1,512]{2,1,0:T(1,128)S(1)} %add_bitcast_fusion), channel_id=1, replica_groups=mesh['tm'=16,'pre'=32] {'tm'}, dimensions={0}, use_global_device_ids=true | all-gather | bytes 34816 | tf_op jit(solution)/shard_map/all_gather | solution.py:9
  195.0 0.9 while.14
  195.9 0.8 add_convert_fusion
  196.8 0.0 all-gather.6.cloned.1.call-update
  196.8 0.0 all-gather.10.cloned.1.call-start
  196.9 21.5 %all-gather.8.cloned.1.call-done = bf16[3072,512]{1,0:T(8,128)(2,1)} async-done(((bf16[192,512]{1,0:T(8,128)(2,1)}), bf16[3072,512]{1,0:T(8,128)(2,1)}) %all-gather.8.cloned.1.call-update) | async-done | bytes 3145744 | tf_op jit(solution)/shard_map/all_gather | solution.py:61
  218.4 2.0 fusion
  220.4 0.0 all-gather.10.cloned.1.call-update
  220.4 42.9 %all-gather.6.cloned.1.call-done = bf16[3072,512]{1,0:T(8,128)(2,1)} async-done(((bf16[192,512]{1,0:T(8,128)(2,1)}), bf16[3072,512]{1,0:T(8,128)(2,1)}) %all-gather.6.cloned.1.call-update) | async-done | bytes 3145744 | tf_op jit(solution)/shard_map/all_gather | solution.py:74
  263.4 96.4 %all-gather.10.cloned.1.call-done = bf16[3072,1024]{1,0:T(8,128)(2,1)} async-done(((bf16[96,1024]{1,0:T(8,128)(2,1)}), bf16[3072,1024]{1,0:T(8,128)(2,1)}) %all-gather.10.cloned.1.call-update) | async-done | bytes 6291472 | tf_op jit(solution)/shard_map/all_gather | solution.py:73
  359.8 8.5 %fusion.19 = f32[512,1024]{1,0:T(8,128)} fusion(bf16[3072,512]{1,0:T(8,128)(2,1)} %all-gather.6.cloned.1.call-done, bf16[3072,1024]{1,0:T(8,128)(2,1)} %all-gather.10.cloned.1.call-done), kind=kOutput, calls=%fused_computation.73 | convolution fusion | flops 3221225472 | bytes 11534336 | tf_op jit(solution)/shard_map/dot_general | solution.py:54
  (128 shorter events, 1.7 us)
Async XLA Ops:
  6.5 211.8 %copy-start = (bf16[1024,512]{1,0:T(8,128)(2,1)S(1)}, bf16[1024,512]{1,0:T(8,128)(2,1)}, u32[]{:S(2)}) copy-start(bf16[1024,512]{1,0:T(8,128)(2,1)} %param.12) | copy-start | bytes 3145732
  6.5 4.6 %copy-start.3 = (f32[512]{0:T(512)S(1)}, f32[512]{0:T(512)}, u32[]{:S(2)}) copy-start(f32[512]{0:T(512)} %param.9) | copy-start | bytes 6148
  6.5 162.2 %all-reduce.30.cloned.1.call-start = ((), (), s32[]{:S(2)}) async-start(), calls=%async_computation.1 | async-start | bytes 786432 | tf_op jit(solution)/shard_map/psum | solution.py:38
  8.8 209.5 %all-gather.8.cloned.1.call-start = ((), (), s32[]{:S(2)}) async-start(), calls=%async_computation.2 | async-start | bytes 3342336 | tf_op jit(solution)/shard_map/all_gather | solution.py:61
  10.6 1.7 copy-start.1
  12.4 0.7 slice-start
  12.7 158.4 %copy-start.4 = (s32[192]{0:T(256)S(1)}, s32[192]{0:T(256)}, u32[]{:S(2)}) copy-start(s32[192]{0:T(256)} %param.13) | copy-start | bytes 2308
  13.3 205.1 %copy-start.2 = (bf16[96,1024]{1,0:T(8,128)(2,1)S(1)}, bf16[96,1024]{1,0:T(8,128)(2,1)}, u32[]{:S(2)}) copy-start(bf16[96,1024]{1,0:T(8,128)(2,1)} %param.10) | copy-start | bytes 589828
  173.0 90.4 %all-gather.6.cloned.1.call-start = ((), (), s32[]{:S(2)}) async-start(), calls=%async_computation | async-start | bytes 3342336 | tf_op jit(solution)/shard_map/all_gather | solution.py:74
  196.8 163.0 %all-gather.10.cloned.1.call-start = ((), (), s32[]{:S(2)}) async-start(), calls=%async_computation.3 | async-start | bytes 6488064 | tf_op jit(solution)/shard_map/all_gather | solution.py:73
Sparse Core Ops, SparseCore 0:
  10.8 157.9 all-reduce.29
  173.1 45.2 all-gather.7
  220.7 42.6 all-gather.5
  266.9 92.9 all-gather.9
where the time goes:
time: 375 us
  waiting for transfers between devices  295 us (79%)
  blocking collectives  42.9 us (11%)
  between operations  13.8 us (4%)
  matrix products  12.8 us (3%)
  other arithmetic  7.6 us (2%)
    psum x1, waiting for transfers between devices, error_rows(): logits = lax.psum(partial_logits, 'pre')  134 us
    all_gather x1, waiting for transfers between devices, shards(): signal_all = lax.all_gather(sources, 'pre', axis=0, tiled=True)  96.4 us
    all_gather x1, waiting for transfers between devices, shards(): lax.all_gather(traces, 'tm', axis=0, tiled=True)  42.9 us
    all_gather x2, blocking collectives, prefix(): everything = jax.tree.map(lambda part: lax.all_gather(part, axis), value)  42.9 us
    all_gather x1, waiting for transfers between devices, shards(): errors_all = lax.all_gather(errors, 'tm', axis=0, tiled=True)  21.5 us
    dot_general x1, matrix products, outer_sum(): lax.dot_general(left_rows, right_rows, (((0,), (0,)), ((), ())), preferre...  8.49 us
  transfers between devices with their start and end apart: 4, of which 4 were waited for; matrix products, arithmetic and copies ran while one was open for 2% of the time, Pallas kernels for 0%

commit v1 on v0

--- a/solution.py
+++ b/solution.py
@@ -2,6 +2,12 @@
 import jax.numpy as jnp
 from jax import lax
 from jax.sharding import PartitionSpec as P
+
+
+def gather_and_add(block, axis):
+    blocks = lax.all_gather(block, axis, axis=0, tiled=False)
+    total = blocks.sum(axis=0)
+    return total
 
 
 def prefix(value, axis, combine, identity):
@@ -35,7 +41,7 @@
     partial_logits = jnp.dot(
         spikes.astype(jnp.bfloat16), readout_weight, preferred_element_type=jnp.float32
     )
-    logits = lax.psum(partial_logits, "pre")
+    logits = gather_and_add(partial_logits, "pre")
     class_prob = jax.nn.softmax(logits, axis=-1)
     classes = lax.broadcasted_iota(jnp.int32, logits.shape, 1)
     onehot = (targets[:, None] == classes).astype(jnp.float32)

time: 375 us -> 346 us (0.923)
  waiting for transfers between devices: 295 us -> 267 us
  blocking collectives: 42.9 us -> 38.9 us
    psum x1 -> x0, waiting for transfers between devices: 134 us -> none  [error_rows(): logits = lax.psum(partial_logits, 'pre')]
    all_gather x0 -> x1, waiting for transfers between devices: none -> 107 us  [gather_and_add(): blocks = lax.all_gather(block, axis, axis=0, tiled=False)]
    reduce_sum x0 -> x1, other arithmetic: none -> 6.01 us  [gather_and_add(): total = blocks.sum(axis=0)]
    all_gather x2, blocking collectives: 42.9 us -> 38.9 us  [prefix(): everything = jax.tree.map(lambda part: lax.all_gather(part, axis), value)]
where the time goes in v1:
time: 346 us; the launch traced here: 345 us
  waiting for transfers between devices  267 us (77%)
  blocking collectives  38.9 us (11%)
  between operations  13.8 us (4%)
  matrix products  12.8 us (4%)
  other arithmetic  10.6 us (3%)
    all_gather x1, waiting for transfers between devices, gather_and_add(): blocks = lax.all_gather(block, axis, axis=0, tiled=False)  107 us
    all_gather x1, waiting for transfers between devices, shards(): signal_all = lax.all_gather(sources, 'pre', axis=0, tiled=True)  96 us
    all_gather x1, waiting for transfers between devices, shards(): lax.all_gather(traces, 'tm', axis=0, tiled=True)  42.7 us
    all_gather x2, blocking collectives, prefix(): everything = jax.tree.map(lambda part: lax.all_gather(part, axis), value)  38.9 us
    all_gather x1, waiting for transfers between devices, shards(): errors_all = lax.all_gather(errors, 'tm', axis=0, tiled=True)  21 us
    dot_general x1, matrix products, outer_sum(): lax.dot_general(left_rows, right_rows, (((0,), (0,)), ((), ())), preferre...  8.49 us
  transfers between devices with their start and end apart: 4, of which 4 were waited for; matrix products, arithmetic and copies ran while one was open for 2% of the time, Pallas kernels for 0%

profile of v1, /device:TPU:1, one launch (start us, length us, event | category | flops | bytes accessed | tf_op | source)
XLA Modules:
  0.0 345.3 jit_solution(13204293994232554518)
XLA Ops:
  6.5 2.3 fusion.3
  8.8 0.0 all-gather.14.cloned.1.call-update
  8.9 0.0 all-gather.10.cloned.1.call-start
  8.9 0.7 broadcast_subtract_fusion
  9.6 1.0 convert_multiply_fusion
  10.7 0.1 slice.194
  10.8 0.1 slice.192
  11.0 0.2 slice.190
  12.9 0.1 fusion.2
  13.0 0.2 slice-done
  13.2 0.1 pad.98
  13.2 0.1 pad.99
  13.3 20.9 %all-gather.1 = f32[16,1,512]{2,1,0:T(1,128)S(1)} all-gather(f32[1,1,512]{2,1,0:T(1,128)S(1)} %add_bitcast_fusion.1), channel_id=1, replica_groups=mesh['tm'=16,'pre'=32] {'tm'}, dimensions={0}, use_global_device_ids=true | all-gather | bytes 34816 | tf_op jit(solution)/shard_map/all_gather | solution.py:15
  34.2 0.1 pad.113
  34.3 0.1 pad.112
  34.4 107.1 %all-gather.14.cloned.1.call-done = f32[6144,512]{1,0:T(8,128)} async-done(((f32[192,512]{1,0:T(8,128)}), f32[6144,512]{1,0:T(8,128)}) %all-gather.14.cloned.1.call-update) | async-done | bytes 12582928 | tf_op jit(solution)/shard_map/all_gather | solution.py:8
  141.4 6.0 %reduce_sum.18 = f32[192,512]{1,0:T(8,128)S(1)} reduce(f32[32,192,512]{2,1,0:T(8,128)} %bitcast.30, f32[]{:T(128)} %constant.37.clone.1), dimensions={0}, to_apply=%region_2.0 | reduce | flops 3047424 | bytes 12976132 | tf_op jit(solution)/shard_map/reduce_sum | solution.py:9
  147.5 0.1 reduce_max.9
  147.6 0.2 fusion.1
  147.8 0.9 subtract_convert_fusion
  148.7 0.0 all-gather.10.cloned.1.call-update
  148.7 0.0 all-gather.8.cloned.1.call-start
  148.8 17.9 %all-gather.2 = f32[16,1,512]{2,1,0:T(1,128)S(1)} all-gather(f32[1,1,512]{2,1,0:T(1,128)S(1)} %add_bitcast_fusion), channel_id=1, replica_groups=mesh['tm'=16,'pre'=32] {'tm'}, dimensions={0}, use_global_device_ids=true | all-gather | bytes 34816 | tf_op jit(solution)/shard_map/all_gather | solution.py:15
  166.7 0.9 while.14
  167.6 0.8 add_convert_fusion
  168.4 0.0 all-gather.8.cloned.1.call-update
  168.5 0.0 all-gather.12.cloned.1.call-start
  168.5 21.0 %all-gather.10.cloned.1.call-done = bf16[3072,512]{1,0:T(8,128)(2,1)} async-done(((bf16[192,512]{1,0:T(8,128)(2,1)}), bf16[3072,512]{1,0:T(8,128)(2,1)}) %all-gather.10.cloned.1.call-update) | async-done | bytes 3145744 | tf_op jit(solution)/shard_map/all_gather | solution.py:67
  189.5 2.0 fusion
  191.6 42.7 %all-gather.8.cloned.1.call-done = bf16[3072,512]{1,0:T(8,128)(2,1)} async-done(((bf16[192,512]{1,0:T(8,128)(2,1)}), bf16[3072,512]{1,0:T(8,128)(2,1)}) %all-gather.8.cloned.1.call-update) | async-done | bytes 3145744 | tf_op jit(solution)/shard_map/all_gather | solution.py:80
  234.3 96.0 %all-gather.12.cloned.1.call-done = bf16[3072,1024]{1,0:T(8,128)(2,1)} async-done(((bf16[96,1024]{1,0:T(8,128)(2,1)}), bf16[3072,1024]{1,0:T(8,128)(2,1)}) %all-gather.12.cloned.1.call-update) | async-done | bytes 6291472 | tf_op jit(solution)/shard_map/all_gather | solution.py:79
  330.3 8.5 %fusion.19 = f32[512,1024]{1,0:T(8,128)} fusion(bf16[3072,512]{1,0:T(8,128)(2,1)} %all-gather.8.cloned.1.call-done, bf16[3072,1024]{1,0:T(8,128)(2,1)} %all-gather.12.cloned.1.call-done), kind=kOutput, calls=%fused_computation.73 | convolution fusion | flops 3221225472 | bytes 11534336 | tf_op jit(solution)/shard_map/dot_general | solution.py:60
  (129 shorter events, 1.7 us)
Async XLA Ops:
  6.5 183.0 %copy-start = (bf16[1024,512]{1,0:T(8,128)(2,1)S(1)}, bf16[1024,512]{1,0:T(8,128)(2,1)}, u32[]{:S(2)}) copy-start(bf16[1024,512]{1,0:T(8,128)(2,1)} %param.12) | copy-start | bytes 3145732
  6.5 4.7 %copy-start.3 = (f32[512]{0:T(512)S(1)}, f32[512]{0:T(512)}, u32[]{:S(2)}) copy-start(f32[512]{0:T(512)} %param.9) | copy-start | bytes 6148
  6.5 134.9 %all-gather.14.cloned.1.call-start = ((), (), s32[]{:S(2)}) async-start(), calls=%async_computation.3 | async-start | bytes 12976128 | tf_op jit(solution)/shard_map/all_gather | solution.py:8
  8.9 180.7 %all-gather.10.cloned.1.call-start = ((), (), s32[]{:S(2)}) async-start(), calls=%async_computation.1 | async-start | bytes 3342336 | tf_op jit(solution)/shard_map/all_gather | solution.py:67
  10.7 1.7 copy-start.1
  12.4 0.7 slice-start
  141.4 6.4 %copy-start.4 = (s32[192]{0:T(256)S(1)}, s32[192]{0:T(256)}, u32[]{:S(2)}) copy-start(s32[192]{0:T(256)} %param.13) | copy-start | bytes 2308
  147.5 42.1 %copy-start.2 = (bf16[96,1024]{1,0:T(8,128)(2,1)S(1)}, bf16[96,1024]{1,0:T(8,128)(2,1)}, u32[]{:S(2)}) copy-start(bf16[96,1024]{1,0:T(8,128)(2,1)} %param.10) | copy-start | bytes 589828
  148.7 85.6 %all-gather.8.cloned.1.call-start = ((), (), s32[]{:S(2)}) async-start(), calls=%async_computation | async-start | bytes 3342336 | tf_op jit(solution)/shard_map/all_gather | solution.py:80
  168.5 161.8 %all-gather.12.cloned.1.call-start = ((), (), s32[]{:S(2)}) async-start(), calls=%async_computation.2 | async-start | bytes 6488064 | tf_op jit(solution)/shard_map/all_gather | solution.py:79
Sparse Core Ops, SparseCore 0:
  10.5 130.8 all-gather.13
  148.8 40.6 all-gather.9
  191.7 42.6 all-gather.7
  237.3 92.9 all-gather.11

commit v2 on v0

--- a/solution.py
+++ b/solution.py
@@ -70,7 +70,15 @@
     traces = (states + powers * incoming[None, :]).astype(jnp.bfloat16)
     offset = lax.axis_index("pre") * pseudo_deriv.shape[0]
     sources = make_signal(errors_all, feedback_weight, pseudo_deriv, offset)
-    signal_all = lax.all_gather(sources, "pre", axis=0, tiled=True)
+    signal_all = jnp.concatenate(
+        lax.all_to_all(
+            jnp.stack([sources for _ in range(lax.psum(1, axis_name="pre"))], axis=0),
+            axis_name="pre",
+            split_axis=0,
+            concat_axis=0,
+        ),
+        axis=0,
+    )
     return outer_sum(lax.all_gather(traces, "tm", axis=0, tiled=True), signal_all)
 
 

time: 375 us -> 393 us (1.048)
  waiting for transfers between devices: 295 us -> 312 us
  blocking collectives: 42.9 us -> 31 us
  starting transfers between devices: 0.13 us -> 10.2 us
    all_gather x1 -> x0, waiting for transfers between devices: 96.4 us -> none  [shards(): signal_all = lax.all_gather(sources, 'pre', axis=0, tiled=True)]
    all_to_all x0 -> x1, waiting for transfers between devices: none -> 65.8 us  [shards(): lax.all_to_all(jnp.stack([sources for _ in range(lax.psum(1, axis_name='p...]
    psum x1, waiting for transfers between devices: 134 us -> 160 us  [error_rows(): logits = lax.psum(partial_logits, 'pre')]
    all_gather x1, waiting for transfers between devices: 21.5 us -> 43.3 us  [shards(): errors_all = lax.all_gather(errors, 'tm', axis=0, tiled=True)]
    all_gather x2, blocking collectives: 42.9 us -> 31 us  [prefix(): everything = jax.tree.map(lambda part: lax.all_gather(part, axis), value)]
    all_to_all x0 -> x1, starting transfers between devices: none -> 10.1 us  [shards(): lax.all_to_all(jnp.stack([sources for _ in range(lax.psum(1, axis_name='p...]
  transfers between devices with their start and end apart: 4 -> 4, of which waited for: 4 -> 4; matrix products, arithmetic and copies ran while one was open for 2% -> 1% of each run, Pallas kernels for 0% -> 0%
where the time goes in v2:
time: 393 us; the launch traced here: 391 us
  waiting for transfers between devices  312 us (79%)
  blocking collectives  31 us (8%)
  between operations  13.8 us (4%)
  matrix products  12.1 us (3%)
  starting transfers between devices  10.2 us (3%)
  other arithmetic  5.93 us (2%)
  local copies, waits for them, and re-layouts  5.03 us (1%)
    psum x1, waiting for transfers between devices, error_rows(): logits = lax.psum(partial_logits, 'pre')  160 us
    all_to_all x1, waiting for transfers between devices, shards(): lax.all_to_all(jnp.stack([sources for _ in range(lax.psum(1, axis_name='p...  65.8 us
    all_gather x1, waiting for transfers between devices, shards(): errors_all = lax.all_gather(errors, 'tm', axis=0, tiled=True)  43.3 us
    all_gather x1, waiting for transfers between devices, shards(): lax.all_gather(traces, 'tm', axis=0, tiled=True)  43 us
    all_gather x2, blocking collectives, prefix(): everything = jax.tree.map(lambda part: lax.all_gather(part, axis), value)  31 us
    all_to_all x1, starting transfers between devices, shards(): lax.all_to_all(jnp.stack([sources for _ in range(lax.psum(1, axis_name='p...  10.1 us
    dot_general x1, matrix products, outer_sum(): lax.dot_general(left_rows, right_rows, (((0,), (0,)), ((), ())), preferre...  8.49 us
  transfers between devices with their start and end apart: 4, of which 4 were waited for; matrix products, arithmetic and copies ran while one was open for 1% of the time, Pallas kernels for 0%

profile of v2, /device:TPU:1, one launch (start us, length us, event | category | flops | bytes accessed | tf_op | source)
XLA Modules:
  0.0 390.6 jit_solution(6858952173470182282)
XLA Ops:
  6.5 2.3 fusion.3
  8.8 0.0 all-reduce.30.cloned.1.call-update
  8.9 0.0 all-gather.7.cloned.1.call-start
  8.9 159.9 %all-reduce.30.cloned.1.call-done = f32[192,512]{1,0:T(8,128)} async-done(((f32[192,512]{1,0:T(8,128)}), f32[192,512]{1,0:T(8,128)}) %all-reduce.30.cloned.1.call-update) | async-done | bytes 393232 | tf_op jit(solution)/shard_map/psum | solution.py:38
  168.8 1.1 reduce_max.9
  169.9 1.2 fusion.1
  171.1 1.9 subtract_convert_fusion
  173.0 0.0 all-gather.7.cloned.1.call-update
  173.1 0.0 copy-start.1
  173.1 0.1 slice.194
  173.2 0.1 slice.192
  173.4 0.2 slice.190
  174.6 0.0 copy-start.3
  175.2 0.1 fusion.2
  175.3 43.3 %all-gather.7.cloned.1.call-done = bf16[3072,512]{1,0:T(8,128)(2,1)} async-done(((bf16[192,512]{1,0:T(8,128)(2,1)}), bf16[3072,512]{1,0:T(8,128)(2,1)}) %all-gather.7.cloned.1.call-update) | async-done | bytes 3145744 | tf_op jit(solution)/shard_map/all_gather | solution.py:61
  218.6 1.3 fusion
  220.0 3.4 stack.2
  223.4 10.1 %all-to-all-start = ((bf16[32,96,1024]{2,1,0:T(8,128)(2,1)}), bf16[32,96,1024]{2,1,0:T(8,128)(2,1)}, u32[]{:S(2)}, u32[]{:S(2)}) async-start(bf16[32,96,1024]{2,1,0:T(8,128)(2,1)} %stack.2), calls=%async_computation | async-start | bytes 12582912 | tf_op jit(solution)/shard_map/all_to_all | solution.py:74
  233.5 0.0 all-gather.5.cloned.1.call-start
  233.6 0.0 slice-done
  233.7 0.1 pad.98
  233.8 0.1 pad.99
  233.8 16.4 %all-gather = f32[16,1,512]{2,1,0:T(1,128)S(1)} all-gather(f32[1,1,512]{2,1,0:T(1,128)S(1)} %add_bitcast_fusion.1), channel_id=1, replica_groups=mesh['tm'=16,'pre'=32] {'tm'}, dimensions={0}, use_global_device_ids=true | all-gather | bytes 34816 | tf_op jit(solution)/shard_map/all_gather | solution.py:9
  250.3 0.1 pad.113
  250.4 0.1 pad.112
  250.4 14.5 %all-gather.1 = f32[16,1,512]{2,1,0:T(1,128)S(1)} all-gather(f32[1,1,512]{2,1,0:T(1,128)S(1)} %add_bitcast_fusion), channel_id=1, replica_groups=mesh['tm'=16,'pre'=32] {'tm'}, dimensions={0}, use_global_device_ids=true | all-gather | bytes 34816 | tf_op jit(solution)/shard_map/all_gather | solution.py:9
  265.0 0.9 while.14
  265.9 0.8 add_convert_fusion
  266.7 0.0 all-gather.5.cloned.1.call-update
  266.8 43.0 %all-gather.5.cloned.1.call-done = bf16[3072,512]{1,0:T(8,128)(2,1)} async-done(((bf16[192,512]{1,0:T(8,128)(2,1)}), bf16[3072,512]{1,0:T(8,128)(2,1)}) %all-gather.5.cloned.1.call-update) | async-done | bytes 3145744 | tf_op jit(solution)/shard_map/all_gather | solution.py:82
  309.8 65.8 %all-to-all-done = bf16[32,96,1024]{2,1,0:T(8,128)(2,1)} async-done(((bf16[32,96,1024]{2,1,0:T(8,128)(2,1)}), bf16[32,96,1024]{2,1,0:T(8,128)(2,1)}, u32[]{:S(2)}, u32[]{:S(2)}) %all-to-all-start) | async-done | bytes 6291488 | tf_op jit(solution)/shard_map/all_to_all | solution.py:74
  375.6 8.5 %fusion.19 = f32[512,1024]{1,0:T(8,128)} fusion(bf16[3072,512]{1,0:T(8,128)(2,1)} %all-gather.5.cloned.1.call-done, bf16[3072,1024]{1,0:T(8,128)(2,1)} %bitcast.11), kind=kOutput, calls=%fused_computation.73 | convolution fusion | flops 3221225472 | bytes 11534336 | tf_op jit(solution)/shard_map/dot_general | solution.py:54
  (128 shorter events, 1.7 us)
Async XLA Ops:
  6.5 212.1 %copy-start = (bf16[1024,512]{1,0:T(8,128)(2,1)S(1)}, bf16[1024,512]{1,0:T(8,128)(2,1)}, u32[]{:S(2)}) copy-start(bf16[1024,512]{1,0:T(8,128)(2,1)} %param.12) | copy-start | bytes 3145732
  6.5 166.5 %copy-start.2 = (s32[192,512]{1,0:T(8,128)S(1)}, s32[192,512]{1,0:T(8,128)}, u32[]{:S(2)}) copy-start(s32[192,512]{1,0:T(8,128)} %param.8) | copy-start | bytes 1179652
  6.5 166.5 %copy-start.4 = (f32[512]{0:T(512)S(1)}, f32[512]{0:T(512)}, u32[]{:S(2)}) copy-start(f32[512]{0:T(512)} %param.9) | copy-start | bytes 6148
  6.5 162.3 %all-reduce.30.cloned.1.call-start = ((), (), s32[]{:S(2)}) async-start(), calls=%async_computation.2 | async-start | bytes 786432 | tf_op jit(solution)/shard_map/psum | solution.py:38
  8.9 209.7 %all-gather.7.cloned.1.call-start = ((), (), s32[]{:S(2)}) async-start(), calls=%async_computation.3 | async-start | bytes 3342336 | tf_op jit(solution)/shard_map/all_gather | solution.py:61
  173.1 1.8 copy-start.1
  174.6 44.0 %copy-start.3 = (bf16[96,1024]{1,0:T(8,128)(2,1)S(1)}, bf16[96,1024]{1,0:T(8,128)(2,1)}, u32[]{:S(2)}) copy-start(bf16[96,1024]{1,0:T(8,128)(2,1)} %param.10) | copy-start | bytes 589828
  223.4 10.2 %slice-start = ((f32[192,512]{1,0:T(8,128)}), f32[1,512]{1,0:T(1,128)S(1)}, s32[]{:S(2)}) async-start(f32[192,512]{1,0:T(8,128)} %copy-done.1), calls=%async_computation.4 | async-start | bytes 4096 | tf_op jit(solution)/shard_map/slice | solution.py:31
  223.4 152.2 %all-to-all-start = ((bf16[32,96,1024]{2,1,0:T(8,128)(2,1)}), bf16[32,96,1024]{2,1,0:T(8,128)(2,1)}, u32[]{:S(2)}, u32[]{:S(2)}) async-start(bf16[32,96,1024]{2,1,0:T(8,128)(2,1)} %stack.2), calls=%async_computation | async-start | bytes 12582912 | tf_op jit(solution)/shard_map/all_to_all | solution.py:74
  233.5 76.3 %all-gather.5.cloned.1.call-start = ((), (), s32[]{:S(2)}) async-start(), calls=%async_computation.1 | async-start | bytes 3342336 | tf_op jit(solution)/shard_map/all_gather | solution.py:82
Sparse Core Ops, SparseCore 0:
  10.8 157.9 all-reduce.29
  173.1 45.4 all-gather.6
  266.9 42.8 all-gather.4
